TPU v7x, 512 devices: a whole 4x8x8 slice. The times are simulated.
512 devices in a mesh: rep: 8 (over y_hi, core), tp: 64 (over x, z, y_lo).
Axes of the slice: x: 4, y: 8 (y_hi: 4, y_lo: 2; y = y_hi * 2 + y_lo), z: 8, core: 2. Of those that a mesh axis runs over, the one named last changes fastest.
Arguments:
- tokens: bfloat16 [4096, 6144], P(('rep', 'tp')), parts along dimension 0, may hold values from -6 to 6
- ln_gain: bfloat16 [6144], replicated, may hold values from 0.5 to 1.5
- ln_bias: bfloat16 [6144], replicated, may hold values from -4 to 4
- w_qkv: bfloat16 [6144, 18432], P(None, 'tp'), may hold values from -0.078125 to 0.078125
- b_qkv: bfloat16 [18432], P('tp'), may hold values from -6 to 6
- w_dense: bfloat16 [6144, 6144], P(None, 'tp'), may hold values from -0.625 to 0.625
- b_dense: bfloat16 [6144], replicated, may hold values from -6 to 6
- prefix_kv: bfloat16 [2, 32, 128, 6144], P(None, 'rep', None, 'tp'), parts along dimension 1, may hold values from -110 to 110
- decode_kv: bfloat16 [2, 256, 16, 6144], P(None, 'rep', None, 'tp'), parts along dimension 1, may hold values from -110 to 110
- prefix_lens: int32 [32], P('rep'), parts along dimension 0, may hold values from 0 to 128, as said below
- span_request: int32 [32], P('rep'), parts along dimension 0, may hold values from 0 to 3, each once
- decode_lens: int32 [256], P('rep'), parts along dimension 0, may hold values from 1 to 16, 256 in all
- slot_valid: int32 [256, 16], P('rep'), parts along dimension 0, may hold values 0 or 1
Outputs:
- layer_out: bfloat16 [4096, 6144], P(('rep', 'tp')), parts along dimension 0
There are 8 independent parts, one for each index of `rep`. A program takes and returns all parts, laid end to end along the dimension named above; an argument that names none is the same for every part. Nothing has to cross between parts.
Inputs may be any that keep to these rules, and one draw needn't show every extreme that they name: `prefix_lens`: some request slot has exactly 128 cached tokens. `span_request`: each request slot is continued by exactly one span. `decode_lens`: the lengths sum to 256 and one equals 16.
All inputs are finite; a program needn't handle non-finite values.
Results may differ from a plain program's by a relative error of at most 0.012.
The roundings to bfloat16 on the way count: a program that leaves them out, or rounds other values in their place, can miss the bound.
Values may be sent and summed in bfloat16 or wider, within the bound.
No kernel may reach another device: no remote copies, remote signals or barrier semaphores. Data moves between devices by JAX's collectives and lax.ppermute only.
A program may use at most 64 MiB of HBM per device.

v0:
```python
import math
import jax
import jax.numpy as jnp
from jax import lax
from jax.sharding import PartitionSpec as P

ROT = 24


def layer_norm(rows, gain, shift):
    value_matrix = rows.astype(jnp.float32)
    center = value_matrix - jnp.mean(value_matrix, axis=-1, keepdims=True)
    spread = jnp.mean(center * center, axis=-1, keepdims=True)
    scaled = center * lax.rsqrt(spread + 1e-05)
    return (scaled * gain.astype(jnp.float32) + shift.astype(jnp.float32)).astype(jnp.bfloat16)


def rotary_tables(places, rot_dims):
    counter = jnp.arange(rot_dims // 2, dtype=jnp.float32)
    inverse = jnp.exp(counter * (-2.0 * math.log(10000.0) / rot_dims))
    angles = places.astype(jnp.float32)[:, None] * inverse[None, :]
    return (jnp.cos(angles), jnp.sin(angles))


def rotate(field, cosine, sine):
    half = cosine.shape[-1]
    first = field[..., :half]
    second = field[..., half : 2 * half]
    return jnp.concatenate(
        [first * cosine - second * sine, second * cosine + first * sine, field[..., 2 * half :]],
        axis=-1,
    )


def token_places(span_lens, cache_lens, span_rows):
    within = jnp.arange(span_rows, dtype=jnp.int32)
    prefill = (span_lens[:, None] + within[None, :]).reshape(-1)
    return jnp.concatenate([prefill, cache_lens])


def batch_stacked(form, left, right):
    return jnp.einsum(form, left, right, preferred_element_type=jnp.float32)


def attend(logit_scores, live, value_matrix):
    peaks = jnp.max(jnp.where(live, logit_scores, -1e30), axis=-1, keepdims=True)
    raised = jnp.where(live, jnp.exp(logit_scores - peaks), 0.0)
    softmax_weights = (raised / jnp.sum(raised, axis=-1, keepdims=True)).astype(jnp.bfloat16)
    return batch_stacked("lsw,lwe->lse", softmax_weights, value_matrix).astype(jnp.bfloat16)


def prefill_attention(
    query, keys, value_matrix, prefix_keys, prefix_vals, span_lens, decode_rows, score_scale
):
    spans = prefix_keys.shape[0]
    slots = prefix_keys.shape[1]
    span_rows = (query.shape[0] - decode_rows) // spans
    prefill_rows = spans * span_rows
    head = query.shape[-1]
    prefill_query_span = query[:prefill_rows].reshape(spans, span_rows, head)
    combined_key_rows = jnp.concatenate(
        [prefix_keys, keys[:prefill_rows].reshape(spans, span_rows, head)], axis=1
    )
    all_vals = jnp.concatenate(
        [prefix_vals, value_matrix[:prefill_rows].reshape(spans, span_rows, head)], axis=1
    )
    logit_scores = (
        batch_stacked("jrf,jyf->jry", prefill_query_span, combined_key_rows) * score_scale
    )
    column = jnp.arange(slots + span_rows, dtype=jnp.int32)[None, None, :]
    row_index = jnp.arange(span_rows, dtype=jnp.int32)[None, :, None]
    live = jnp.where(column < slots, column < span_lens[:, None, None], column - slots <= row_index)
    return attend(logit_scores, live, all_vals).reshape(prefill_rows, head)


def decode_attention(
    query, keys, value_matrix, stored_key_cache, cache_vals, cache_lens, slot_valid, score_scale
):
    decode_rows = stored_key_cache.shape[0]
    slots = stored_key_cache.shape[1]
    first_row = query.shape[0] - decode_rows
    decode_query_row = query[first_row:]
    own_keys = keys[first_row:]
    own_vals = value_matrix[first_row:]
    cache_present = (
        batch_stacked("jrf,jyf->jry", decode_query_row[:, None, :], stored_key_cache) * score_scale
    )
    itself = (
        jnp.sum(decode_query_row.astype(jnp.float32) * own_keys.astype(jnp.float32), axis=-1)[
            :, None, None
        ]
        * score_scale
    )
    logit_scores = jnp.concatenate([cache_present, itself], axis=-1)
    column = jnp.arange(slots, dtype=jnp.int32)[None, :]
    live_cache = (column < cache_lens[:, None]) & (slot_valid == 1)
    live = jnp.concatenate([live_cache, jnp.ones((decode_rows, 1), dtype=bool)], axis=-1)[
        :, None, :
    ]
    all_vals = jnp.concatenate([cache_vals, own_vals[:, None, :]], axis=1)
    return attend(logit_scores, live, all_vals)[:, 0, :]


def on_device(
    tokens,
    ln_gain,
    ln_bias,
    w_qkv,
    b_qkv,
    w_dense,
    b_dense,
    prefix_kv,
    decode_kv,
    prefix_lens,
    span_request,
    decode_lens,
    slot_valid,
):
    normed = layer_norm(tokens, ln_gain, ln_bias)
    joined = jnp.dot(
        lax.all_gather(normed, "tp", axis=0, tiled=True), w_qkv, preferred_element_type=jnp.float32
    )
    joined = joined + b_qkv.astype(jnp.float32)
    head = joined.shape[1] // 3
    token_count = joined.shape[0]
    spans = prefix_kv.shape[1]
    decode_rows = decode_kv.shape[1]
    span_rows = (token_count - decode_rows) // spans
    span_lens = jnp.take(prefix_lens, span_request, axis=0)
    cosine, sine = rotary_tables(token_places(span_lens, decode_lens, span_rows), ROT)
    query = rotate(joined[:, :head], cosine, sine).astype(jnp.bfloat16)
    keys = rotate(joined[:, head : 2 * head], cosine, sine).astype(jnp.bfloat16)
    value_matrix = joined[:, 2 * head :].astype(jnp.bfloat16)
    prefix_keys = jnp.take(prefix_kv[0], span_request, axis=0)
    prefix_vals = jnp.take(prefix_kv[1], span_request, axis=0)
    score_scale = 1.0 / math.sqrt(head)
    early = prefill_attention(
        query, keys, value_matrix, prefix_keys, prefix_vals, span_lens, decode_rows, score_scale
    )
    late = decode_attention(
        query, keys, value_matrix, decode_kv[0], decode_kv[1], decode_lens, slot_valid, score_scale
    )
    heads_out = jnp.concatenate([early, late], axis=0)
    mixed = jnp.dot(
        lax.all_gather(heads_out, "tp", axis=1, tiled=True),
        w_dense,
        preferred_element_type=jnp.float32,
    )
    own_rows = lax.all_to_all(mixed, "tp", split_axis=0, concat_axis=1, tiled=True)
    attn = (own_rows + b_dense.astype(jnp.float32)).astype(jnp.bfloat16)
    return (attn.astype(jnp.float32) + tokens.astype(jnp.float32)).astype(jnp.bfloat16)


def solution(mesh):
    placed = (
        P(("rep", "tp"), None),
        P(),
        P(),
        P(None, "tp"),
        P("tp"),
        P(None, "tp"),
        P(),
        P(None, "rep", None, "tp"),
        P(None, "rep", None, "tp"),
        P("rep"),
        P("rep"),
        P("rep"),
        P("rep", None),
    )
    return jax.shard_map(
        on_device, mesh=mesh, in_specs=placed, out_specs=P(("rep", "tp"), None), check_vma=False
    )
```

profile of v0, /device:TPU:8, one launch (start us, length us, event | category | flops | bytes accessed | tf_op | source)
XLA Modules:
  0.0 731.0 jit_solution(18445028543384354713)
XLA Ops:
  6.5 0.9 convert_element_type.60
  7.4 0.9 convert_element_type.59
  8.3 1.1 convert_reduce_fusion
  9.4 1.1 fusion.12
  10.5 1.6 fusion.15
  12.1 0.0 all-gather.3.cloned.1.call-update
  12.2 0.0 all-gather.5.cloned.1.call-start
  12.2 1.3 convert_element_type.62
  13.5 0.7 compare_select_fusion
  14.1 1.3 gather_fusion
  15.4 0.7 broadcast_select_fusion.2
  16.1 0.6 copy-done.3
  16.7 0.1 iota_add_fusion
  16.7 0.1 add.82
  16.8 1.6 slice_bitcast_fusion.1
  18.5 2.1 gather_fusion.2
  20.5 2.1 gather_fusion.1
  22.6 0.6 multiply_exponential_fusion
  23.2 0.5 iota_compare_fusion.3
  23.7 0.7 add_convert_fusion.1
  24.5 1.3 iota_compare_fusion.2
  25.8 1.3 fusion.44
  27.1 0.6 iota_compare_fusion
  27.7 1.6 slice_bitcast_fusion
  29.3 1.7 broadcast_select_fusion
  31.0 305.6 %all-gather.3.cloned.1.call-done = bf16[512,6144]{1,0:T(8,128)(2,1)} async-done(((bf16[8,6144]{1,0:T(8,128)(2,1)}), bf16[512,6144]{1,0:T(8,128)(2,1)}) %all-gather.3.cloned.1.call-update) | async-done | bytes 6291472 | tf_op jit(solution)/shard_map/all_gather | solution.py:121
  336.5 4.8 fusion.55
  341.3 0.7 slice_bitcast_fusion.3
  342.1 0.2 fusion.37
  342.3 0.7 multiply_reduce_fusion.2
  343.0 0.7 pad_maximum_fusion
  343.7 0.6 slice.92
  344.3 1.4 copy.29
  345.7 0.6 multiply_bitcast_fusion
  346.3 1.5 copy.43
  347.8 1.1 multiply_reduce_fusion.1
  348.8 0.7 copy.36
  349.5 0.7 broadcast_multiply_fusion
  350.2 0.7 select_reduce_fusion.1
  350.9 0.7 fusion.45
  351.6 1.3 fusion.46
  352.9 0.8 copy.44
  353.7 1.7 multiply_reduce_fusion
  355.4 1.4 copy.40
  356.8 1.6 reshape.178
  358.4 1.5 copy.25
  360.0 1.6 reshape.177
  361.6 1.6 reshape.179
  363.3 1.5 copy.27
  364.8 1.2 convolution_multiply_fusion
  366.1 0.8 copy-done.1
  366.8 1.1 fusion.56
  368.0 2.9 convolution_convert_fusion
  370.9 1.6 copy.28
  372.4 1.7 reshape.180
  374.1 1.6 pad_maximum_fusion.2
  375.7 317.5 %all-gather.5.cloned.1.call-done = bf16[512,6144]{0,1:T(8,128)(2,1)} async-done(((bf16[512,96]{0,1:T(8,128)(2,1)}), bf16[512,6144]{0,1:T(8,128)(2,1)}) %all-gather.5.cloned.1.call-update) | async-done | bytes 6291472 | tf_op jit(solution)/shard_map/all_gather | solution.py:145
  693.3 5.6 convolution_bitcast_fusion
  698.9 9.1 %all-to-all-start = ((f32[64,8,96]{2,1,0:T(8,128)}), f32[64,8,96]{2,1,0:T(8,128)}, u32[]{:S(2)}, u32[]{:S(2)}) async-start(f32[64,8,96]{2,1,0:T(8,128)} %convolution_bitcast_fusion), calls=%async_computation | async-start | bytes 524288 | tf_op jit(solution)/shard_map/all_to_all | solution.py:149
  708.0 0.6 convert_element_type.70
  708.6 10.4 %all-to-all-done = f32[64,8,96]{2,1,0:T(8,128)} async-done(((f32[64,8,96]{2,1,0:T(8,128)}), f32[64,8,96]{2,1,0:T(8,128)}, u32[]{:S(2)}, u32[]{:S(2)}) %all-to-all-start) | async-done | bytes 196640 | tf_op jit(solution)/shard_map/all_to_all | solution.py:149
  719.0 1.7 copy.31
  720.7 1.8 all_to_all.17
  722.5 1.7 fusion.16
  (15 shorter events, 0.1 us)
Async XLA Ops:
  6.5 330.0 %copy-start = (bf16[6144,288]{0,1:T(8,128)(2,1)S(1)}, bf16[6144,288]{0,1:T(8,128)(2,1)}, u32[]{:S(2)}) copy-start(bf16[6144,288]{0,1:T(8,128)(2,1)} %param.18) | copy-start | bytes 10616836
  6.5 330.0 %all-gather.3.cloned.1.call-start = ((), (), s32[]{:S(2)}) async-start(), calls=%async_computation.1 | async-start | bytes 6389760 | tf_op jit(solution)/shard_map/all_gather | solution.py:121
  12.2 681.1 %all-gather.5.cloned.1.call-start = ((), (), s32[]{:S(2)}) async-start(), calls=%async_computation.2 | async-start | bytes 6389760 | tf_op jit(solution)/shard_map/all_gather | solution.py:145
  16.1 0.6 copy-start.3
  31.0 311.1 %copy-start.4 = (f32[12]{0:T(128)S(1)}, f32[12]{0:T(128)}, u32[]{:S(2)}) copy-start(f32[12]{0:T(128)} %multiply_exponential_fusion) | copy-start | bytes 148
  366.1 0.8 copy-start.1
  367.9 340.0 %copy-start.2 = (bf16[6144]{0:T(1024)(128)(2,1)S(1)}, bf16[6144]{0:T(1024)(128)(2,1)}, u32[]{:S(2)}) copy-start(bf16[6144]{0:T(1024)(128)(2,1)} %param.21) | copy-start | bytes 36868
  698.9 20.1 %all-to-all-start = ((f32[64,8,96]{2,1,0:T(8,128)}), f32[64,8,96]{2,1,0:T(8,128)}, u32[]{:S(2)}, u32[]{:S(2)}) async-start(f32[64,8,96]{2,1,0:T(8,128)} %convolution_bitcast_fusion), calls=%async_computation | async-start | bytes 524288 | tf_op jit(solution)/shard_map/all_to_all | solution.py:149
Sparse Core Ops, SparseCore 0:
  12.3 324.1 all-gather.2
  375.9 317.3 all-gather.4
where the time goes:
time: 732 us; the launch traced here: 731 us
  waiting for transfers between devices  634 us (87%)
  local copies, waits for them, and re-layouts  31.8 us (4%)
  other arithmetic  28.4 us (4%)
  matrix products  14.6 us (2%)
  between operations  13.5 us (2%)
  starting transfers between devices  9.13 us (1%)
    all_gather x1, waiting for transfers between devices, on_device(): lax.all_gather(heads_out, 'tp', axis=1, tiled=True)  318 us
    all_gather x1, waiting for transfers between devices, on_device(): lax.all_gather(normed, 'tp', axis=0, tiled=True)  306 us
  transfers between devices with their start and end apart: 3, of which 3 were waited for; matrix products, arithmetic and copies ran while one was open for 3% of the time, Pallas kernels for 0%

commit v1 on v0

--- a/solution.py
+++ b/solution.py
@@ -117,9 +117,14 @@
     slot_valid,
 ):
     normed = layer_norm(tokens, ln_gain, ln_bias)
-    joined = jnp.dot(
-        lax.all_gather(normed, "tp", axis=0, tiled=True), w_qkv, preferred_element_type=jnp.float32
-    )
+
+    def set_sector_by_axis(shard_in):
+        base_arr = lax.psum(1, axis_name="tp")
+        even = jnp.stack([shard_in] * base_arr, 0)
+        h_now = lax.all_to_all(even, axis_name="tp", split_axis=0, concat_axis=0)
+        return jnp.concatenate(h_now, 0)
+
+    joined = jnp.dot(set_sector_by_axis(normed), w_qkv, preferred_element_type=jnp.float32)
     joined = joined + b_qkv.astype(jnp.float32)
     head = joined.shape[1] // 3
     token_count = joined.shape[0]

time: 732 us -> 572 us (0.78)
  waiting for transfers between devices: 634 us -> 456 us
  starting transfers between devices: 9.13 us -> 24.2 us
    all_gather x1 -> x0, waiting for transfers between devices: 306 us -> none  [on_device(): lax.all_gather(normed, 'tp', axis=0, tiled=True)]
    all_to_all x0 -> x1, waiting for transfers between devices: none -> 128 us  [set_sector_by_axis(): h_now = lax.all_to_all(even, axis_name='tp', split_axis=0, concat_axis=0)]
    all_to_all x0 -> x1, starting transfers between devices: none -> 15.1 us  [set_sector_by_axis(): h_now = lax.all_to_all(even, axis_name='tp', split_axis=0, concat_axis=0)]
where the time goes in v1:
time: 572 us; the launch traced here: 571 us
  waiting for transfers between devices  456 us (80%)
  local copies, waits for them, and re-layouts  35.4 us (6%)
  other arithmetic  27.4 us (5%)
  starting transfers between devices  24.2 us (4%)
  matrix products  14.6 us (3%)
  between operations  13.5 us (2%)
    all_gather x1, waiting for transfers between devices, on_device(): lax.all_gather(heads_out, 'tp', axis=1, tiled=True)  317 us
    all_to_all x1, waiting for transfers between devices, set_sector_by_axis(): h_now = lax.all_to_all(even, axis_name='tp', split_axis=0, concat_axis=0)  128 us
    all_to_all x1, starting transfers between devices, set_sector_by_axis(): h_now = lax.all_to_all(even, axis_name='tp', split_axis=0, concat_axis=0)  15.1 us
  transfers between devices with their start and end apart: 3, of which 3 were waited for; matrix products, arithmetic and copies ran while one was open for 3% of the time, Pallas kernels for 0%

profile of v1, /device:TPU:8, one launch (start us, length us, event | category | flops | bytes accessed | tf_op | source)
XLA Modules:
  0.0 570.6 jit_solution(8564756677092287265)
XLA Ops:
  6.5 0.9 convert_element_type.60
  7.4 0.9 convert_element_type.59
  8.3 1.1 convert_reduce_fusion
  9.4 1.1 fusion.17
  10.5 1.0 fusion.20
  11.5 3.4 stack.2
  14.9 15.1 %all-to-all-start = ((bf16[64,8,6144]{2,1,0:T(8,128)(2,1)}), bf16[64,8,6144]{2,1,0:T(8,128)(2,1)}, u32[]{:S(2)}, u32[]{:S(2)}) async-start(bf16[64,8,6144]{2,1,0:T(8,128)(2,1)} %stack.2), calls=%async_computation | async-start | bytes 12582912 | tf_op jit(solution)/shard_map/all_to_all | solution.py:124
  30.1 0.5 convert_element_type.62
  30.6 0.7 compare_select_fusion
  31.3 1.1 gather_fusion
  32.4 1.2 broadcast_select_fusion.2
  33.6 0.6 copy-done.6
  34.2 0.1 iota_add_fusion
  34.3 0.1 add.82
  34.4 1.6 slice_bitcast_fusion.1
  36.0 2.2 gather_fusion.2
  38.2 2.2 gather_fusion.1
  40.4 0.5 multiply_exponential_fusion
  41.0 0.5 iota_compare_fusion.3
  41.5 0.7 add_convert_fusion.1
  42.3 1.3 iota_compare_fusion.2
  43.6 1.2 fusion.49
  44.8 0.6 iota_compare_fusion
  45.4 1.6 slice_bitcast_fusion
  47.0 1.7 broadcast_select_fusion
  48.7 127.9 %all-to-all-done = bf16[64,8,6144]{2,1,0:T(8,128)(2,1)} async-done(((bf16[64,8,6144]{2,1,0:T(8,128)(2,1)}), bf16[64,8,6144]{2,1,0:T(8,128)(2,1)}, u32[]{:S(2)}, u32[]{:S(2)}) %all-to-all-start) | async-done | bytes 6291488 | tf_op jit(solution)/shard_map/all_to_all | solution.py:124
  176.6 4.8 fusion.60
  181.4 0.7 slice_bitcast_fusion.3
  182.2 0.2 fusion.42
  182.4 0.7 multiply_reduce_fusion.2
  183.1 0.7 pad_maximum_fusion
  183.8 0.6 slice.92
  184.4 1.4 copy.29
  185.8 0.6 multiply_bitcast_fusion
  186.4 1.5 copy.43
  187.9 1.1 multiply_reduce_fusion.1
  188.9 0.7 copy.36
  189.6 0.7 broadcast_multiply_fusion
  190.3 0.7 select_reduce_fusion.1
  191.0 0.7 fusion.50
  191.7 1.3 fusion.51
  193.0 0.8 copy.44
  193.7 1.7 multiply_reduce_fusion
  195.4 1.4 copy.40
  196.8 1.6 reshape.184
  198.5 1.5 copy.25
  200.0 1.6 reshape.183
  201.7 1.6 reshape.185
  203.3 1.5 copy.27
  204.8 1.2 convolution_multiply_fusion
  206.1 0.8 copy-done.2
  206.9 1.1 fusion.61
  208.0 2.9 convolution_convert_fusion
  210.9 1.6 copy.28
  212.5 1.7 reshape.186
  214.1 1.6 pad_maximum_fusion.2
  215.8 317.1 %all-gather.2.cloned.1.call-done = bf16[512,6144]{0,1:T(8,128)(2,1)} async-done(((bf16[512,96]{0,1:T(8,128)(2,1)}), bf16[512,6144]{0,1:T(8,128)(2,1)}) %all-gather.2.cloned.1.call-update) | async-done | bytes 6291472 | tf_op jit(solution)/shard_map/all_gather | solution.py:150
  532.9 5.6 convolution_bitcast_fusion
  538.5 9.1 %all-to-all-start.1 = ((f32[64,8,96]{2,1,0:T(8,128)}), f32[64,8,96]{2,1,0:T(8,128)}, u32[]{:S(2)}, u32[]{:S(2)}) async-start(f32[64,8,96]{2,1,0:T(8,128)} %convolution_bitcast_fusion), calls=%async_computation.1 | async-start | bytes 524288 | tf_op jit(solution)/shard_map/all_to_all | solution.py:154
  547.6 0.6 convert_element_type.70
  548.2 10.4 %all-to-all-done.1 = f32[64,8,96]{2,1,0:T(8,128)} async-done(((f32[64,8,96]{2,1,0:T(8,128)}), f32[64,8,96]{2,1,0:T(8,128)}, u32[]{:S(2)}, u32[]{:S(2)}) %all-to-all-start.1) | async-done | bytes 196640 | tf_op jit(solution)/shard_map/all_to_all | solution.py:154
  558.7 1.7 copy.31
  560.4 1.8 all_to_all.21
  562.1 1.7 fusion.21
  (23 shorter events, 0.1 us)
Async XLA Ops:
  6.5 170.1 %copy-start = (bf16[6144,288]{0,1:T(8,128)(2,1)S(1)}, bf16[6144,288]{0,1:T(8,128)(2,1)}, u32[]{:S(2)}) copy-start(bf16[6144,288]{0,1:T(8,128)(2,1)} %param.18) | copy-start | bytes 10616836
  14.9 15.2 %copy-start.7 = (bf16[288]{0:T(512)(128)(2,1)S(1)}, bf16[288]{0:T(512)(128)(2,1)}, u32[]{:S(2)}) copy-start(bf16[288]{0:T(512)(128)(2,1)} %param.19) | copy-start | bytes 1732
  14.9 16.4 %copy-start.1 = (s32[4]{0:T(128)S(1)}, s32[4]{0:T(128)}, u32[]{:S(2)}) copy-start(s32[4]{0:T(128)} %param.24) | copy-start | bytes 52
  14.9 28.7 %copy-start.4 = (s32[32,16]{0,1:T(8,128)S(1)}, s32[32,16]{0,1:T(8,128)}, u32[]{:S(2)}) copy-start(s32[32,16]{0,1:T(8,128)} %param.27) | copy-start | bytes 6148
  14.9 161.7 %all-to-all-start = ((bf16[64,8,6144]{2,1,0:T(8,128)(2,1)}), bf16[64,8,6144]{2,1,0:T(8,128)(2,1)}, u32[]{:S(2)}, u32[]{:S(2)}) async-start(bf16[64,8,6144]{2,1,0:T(8,128)(2,1)} %stack.2), calls=%async_computation | async-start | bytes 12582912 | tf_op jit(solution)/shard_map/all_to_all | solution.py:124
  30.0 502.9 %all-gather.2.cloned.1.call-start = ((), (), s32[]{:S(2)}) async-start(), calls=%async_computation.2 | async-start | bytes 6389760 | tf_op jit(solution)/shard_map/all_gather | solution.py:150
  31.3 2.3 copy-start.5
  33.6 0.6 copy-start.6
  48.7 133.5 %copy-start.8 = (f32[12]{0:T(128)S(1)}, f32[12]{0:T(128)}, u32[]{:S(2)}) copy-start(f32[12]{0:T(128)} %multiply_exponential_fusion) | copy-start | bytes 148
  206.1 0.8 copy-start.2
  208.0 339.6 %copy-start.3 = (bf16[6144]{0:T(1024)(128)(2,1)S(1)}, bf16[6144]{0:T(1024)(128)(2,1)}, u32[]{:S(2)}) copy-start(bf16[6144]{0:T(1024)(128)(2,1)} %param.21) | copy-start | bytes 36868
  538.5 20.1 %all-to-all-start.1 = ((f32[64,8,96]{2,1,0:T(8,128)}), f32[64,8,96]{2,1,0:T(8,128)}, u32[]{:S(2)}, u32[]{:S(2)}) async-start(f32[64,8,96]{2,1,0:T(8,128)} %convolution_bitcast_fusion), calls=%async_computation.1 | async-start | bytes 524288 | tf_op jit(solution)/shard_map/all_to_all | solution.py:154
Sparse Core Ops, SparseCore 0:
  215.9 316.9 all-gather.1
